TPU v7x, 32 devices: a whole 2x2x4 slice. The times are simulated.
32 devices in a mesh: groups: 2 (over x), seq: 16 (over z, y, core).
Axes of the slice: x: 2, y: 2, z: 4, core: 2. Of those that a mesh axis runs over, the one named last changes fastest.
Arguments:
- clean: bfloat16 [8192, 2048], P(('groups', 'seq')), parts along dimension 0, may hold values from -6 to 6
- delta: bfloat16 [8192, 2048], P(('groups', 'seq')), parts along dimension 0, may hold values from -0.25 to 0.25
- cotangent: bfloat16 [8192, 1024], P(('groups', 'seq')), parts along dimension 0, may hold values from -6 to 6
- w_query: bfloat16 [2048, 1024], P('seq'), may hold values from -0.125 to 0.125
- w_key: bfloat16 [2048, 1024], P('seq'), may hold values from -0.125 to 0.125
- w_value: bfloat16 [2048, 1024], P('seq'), may hold values from -0.125 to 0.125
- masks: int32 [32, 2, 2], P(('groups', 'seq')), parts along dimension 0, may hold values 0 or 1
Outputs:
- output: bfloat16 [8192, 1024], P(('groups', 'seq')), parts along dimension 0
- grad_input: bfloat16 [8192, 2048], P(('groups', 'seq')), parts along dimension 0
There are 2 independent parts, one for each index of `groups`. A program takes and returns all parts, laid end to end along the dimension named above; an argument that names none is the same for every part. Nothing has to cross between parts.
All inputs are finite; a program needn't handle non-finite values. No bound on the sum of `masks` on one device may be relied on, other than what follows from the above.
Results may differ from a plain program's by a relative error of at most 0.012.
Values may be sent and summed in bfloat16 or wider, within the bound.
No kernel may reach another device: no remote copies, remote signals or barrier semaphores. Data moves between devices by JAX's collectives and lax.ppermute only.
A program may use at most 128 MiB of HBM per device.

v0:
```python
import jax
import jax.numpy as jnp
from jax import lax
from jax.sharding import PartitionSpec as P

NH = 8
DH = 128
BLK = 128
EPSILON = 1e-06


def carried_in(shard, axis, combine, identity, reverse):
    peers, index = (lax.axis_size(axis), lax.axis_index(axis))
    everything = lax.all_gather(shard, axis)
    start = jnp.broadcast_to(jnp.asarray(identity, shard.dtype), shard.shape)

    def turn(k, before):
        at = peers - 1 - k if reverse else k
        reached = at > index if reverse else at < index
        new = combine(before, everything[at])
        return jnp.where(reached, new, before)

    return lax.fori_loop(0, peers, turn, start)


def allowed_pairs(blocks, width):
    count = blocks.shape[0]
    row = jnp.arange(count)[:, None]
    col = jnp.arange(count)[None, :]
    inner_row = jnp.arange(width)[:, None]
    inner_col = jnp.arange(width)[None, :]
    lower = (row > col).astype(jnp.float32)[:, :, None, None]
    same = (row == col).astype(jnp.float32)[:, :, None, None] * (inner_row >= inner_col).astype(
        jnp.float32
    )[None, None]
    return blocks.astype(jnp.float32)[:, :, None, None] * (lower + same)


def add_states(earlier, later_one):
    return earlier + later_one


def on_device(clean, delta, cotangent, w_query, w_key, w_value, masks):
    tok_rows = clean.shape[0]
    features = w_query.shape[1]
    blocks_here = tok_rows // BLK
    f32 = jnp.float32
    x_in = (clean.astype(f32) + delta.astype(f32)).astype(jnp.bfloat16)
    w_cat = jnp.concatenate([w_query, w_key, w_value], axis=1)
    full_weights = lax.all_gather(w_cat, "seq", axis=0, tiled=True)
    projected = jnp.dot(x_in, full_weights, preferred_element_type=f32)
    projected = projected.astype(jnp.bfloat16)
    query = projected[:, :features].reshape(blocks_here, BLK, NH, DH)
    key = projected[:, features : 2 * features].reshape(blocks_here, BLK, NH, DH)
    value = projected[:, 2 * features :].reshape(blocks_here, BLK, NH, DH)
    zero_state = jnp.zeros((NH, DH, DH), f32)
    state_local = jnp.einsum("ibhd,ibhe->hde", key, value, preferred_element_type=f32)
    state = carried_in(state_local, "seq", add_states, zero_state, False)
    state_b = state.astype(jnp.bfloat16)
    allow = allowed_pairs(masks[0], BLK)
    scores = jnp.einsum("ibhd,jchd->hijbc", query, key, preferred_element_type=f32)
    attn = (scores * allow).astype(jnp.bfloat16)
    mixed = jnp.einsum("hijbc,jchd->ibhd", attn, value, preferred_element_type=f32)
    mixed = mixed + jnp.einsum("ibhd,hde->ibhe", query, state_b, preferred_element_type=f32)
    root = jnp.sqrt(jnp.mean(mixed * mixed, axis=-1, keepdims=True) + EPSILON)
    normed = mixed / root
    output = normed.astype(jnp.bfloat16).reshape(tok_rows, features)
    grad_out = cotangent.astype(f32).reshape(blocks_here, BLK, NH, DH)
    d_mixed = (grad_out - normed * jnp.mean(grad_out * normed, axis=-1, keepdims=True)) / root
    d_mixed_b = d_mixed.astype(jnp.bfloat16)
    grad_local = jnp.einsum("ibhd,ibhe->hde", query, d_mixed_b, preferred_element_type=f32)
    later = carried_in(grad_local, "seq", add_states, zero_state, True)
    later_b = later.astype(jnp.bfloat16)
    d_attn = (
        jnp.einsum("ibhe,jche->hijbc", d_mixed_b, value, preferred_element_type=f32) * allow
    ).astype(jnp.bfloat16)
    d_query = jnp.einsum("hijbc,jchd->ibhd", d_attn, key, preferred_element_type=f32)
    d_query = d_query + jnp.einsum("ibhe,hde->ibhd", d_mixed_b, state_b, preferred_element_type=f32)
    d_key = jnp.einsum("hijbc,ibhd->jchd", d_attn, query, preferred_element_type=f32)
    d_key = d_key + jnp.einsum("jche,hde->jchd", value, later_b, preferred_element_type=f32)
    d_value = jnp.einsum("hijbc,ibhe->jche", attn, d_mixed_b, preferred_element_type=f32)
    d_value = d_value + jnp.einsum("jchd,hde->jche", key, later_b, preferred_element_type=f32)
    d_proj = jnp.concatenate(
        [
            d_query.reshape(tok_rows, features),
            d_key.reshape(tok_rows, features),
            d_value.reshape(tok_rows, features),
        ],
        axis=1,
    ).astype(jnp.bfloat16)
    grad_input = lax.dot_general(
        d_proj, full_weights, (((1,), (1,)), ((), ())), preferred_element_type=f32
    )
    return (output, grad_input.astype(jnp.bfloat16))


def solution(mesh):
    return jax.shard_map(
        on_device,
        mesh=mesh,
        in_specs=(
            P(("groups", "seq"), None),
            P(("groups", "seq"), None),
            P(("groups", "seq"), None),
            P("seq", None),
            P("seq", None),
            P("seq", None),
            P(("groups", "seq"), None, None),
        ),
        out_specs=(P(("groups", "seq"), None), P(("groups", "seq"), None)),
        check_vma=False,
    )
```

profile of v0, /device:TPU:0, one launch (start us, length us, event | category | flops | bytes accessed | tf_op | source)
XLA Modules:
  0.0 334.4 jit_solution(9458282480844987957)
XLA Ops:
  7.2 2.2 pad_maximum_fusion
  9.5 104.9 %all-gather.6.cloned.1.call-done = bf16[2048,3072]{1,0:T(8,128)(2,1)} async-done(((bf16[128,3072]{1,0:T(8,128)(2,1)}), bf16[2048,3072]{1,0:T(8,128)(2,1)}) %all-gather.6.cloned.1.call-update) | async-done | bytes 12582928 | tf_op jit(solution)/shard_map/all_gather | solution.py:50
  114.4 8.0 %convolution_convert_fusion = bf16[256,3072]{1,0:T(8,128)(2,1)S(1)} fusion(bf16[2048,3072]{1,0:T(8,128)(2,1)} %all-gather.6.cloned.1.call-done, bf16[256,2048]{1,0:T(8,128)(2,1)S(1)} %copy-done.12, bf16[256,2048]{1,0:T(8,128)(2,1)S(1)} %copy-done.13), kind=kOutput, calls=%fused_computation.2 | convolution fusion | flops 3224109056 | bytes 16252928 | tf_op jit(solution)/shard_map/dot_general | solution.py:51
  126.6 1.6 copy.70
  130.0 1.4 copy.101
  132.3 2.1 copy.96
  134.4 2.1 copy.79
  136.6 1.7 fusion.1
  139.3 1.3 convolution_bitcast_fusion
  140.6 56.5 %all-gather.8.cloned.1.call-done = f32[128,128,128]{2,1,0:T(8,128)} async-done(((f32[8,128,128]{2,1,0:T(8,128)}), f32[128,128,128]{2,1,0:T(8,128)}) %all-gather.8.cloned.1.call-update) | async-done | bytes 8388624 | tf_op jit(solution)/shard_map/all_gather | solution.py:14
  197.1 20.1 %while.30 = (s32[]{:T(128)}, f32[8,128,128]{2,1,0:T(8,128)S(1)}, s32[]{:T(128)}, f32[16,8,128,128]{3,2,1,0:T(8,128)}, s32[]{:T(128)}, /*index=5*/s32[]{:T(128)}) while((s32[]{:T(128)}, f32[8,128,128]{2,1,0:T(8,128)S(1)}, s32[]{:T(128)}, f32[16,8,128,128]{3,2,1,0:T(8,128)}, s32[]{:T(128)}, /*index=5*/s32[]{:T(128)}) %tuple.88), condition=%wide.region_1.2_spmd.clone, body=%wide.region_0.1_spmd.clone.sunk | while | flops 393220 | bytes 1572957 | solution.py:23
  197.1 1.3 add_select_fusion.4
  217.2 1.6 multiply_reduce_fusion.1
  221.3 1.5 fusion
  222.7 1.4 convolution_bitcast_fusion.3
  225.2 2.2 copy.76
  227.3 2.0 copy.159
  229.3 2.1 copy.68
  231.4 2.0 copy.160
  233.4 1.4 convolution_bitcast_fusion.2
  235.4 59.2 %all-gather.10.cloned.1.call-done = f32[128,128,128]{2,1,0:T(8,128)} async-done(((f32[8,128,128]{2,1,0:T(8,128)}), f32[128,128,128]{2,1,0:T(8,128)}) %all-gather.10.cloned.1.call-update) | async-done | bytes 8388624 | tf_op jit(solution)/shard_map/all_gather | solution.py:14
  294.5 20.2 %while.31 = (s32[]{:T(128)}, f32[8,128,128]{2,1,0:T(8,128)S(1)}, s32[]{:T(128)}, f32[16,8,128,128]{3,2,1,0:T(8,128)}, s32[]{:T(128)}, /*index=5*/s32[]{:T(128)}, s32[]{:T(128)}, s32[]{:T(128)}) while((s32[]{:T(128)}, f32[8,128,128]{2,1,0:T(8,128)S(1)}, s32[]{:T(128)}, f32[16,8,128,128]{3,2,1,0:T(8,128)}, s32[]{:T(128)}, ...), condition=%wide.region_5.6_spmd.clone, body=%wide.region_4.5_spmd.clone.sunk | while | flops 393224 | bytes 1573019 | solution.py:23
  314.7 1.5 fusion.12
  318.9 9.0 %convolution_convert_fusion.1 = bf16[256,2048]{1,0:T(8,128)(2,1)} fusion(bf16[2048,3072]{1,0:T(8,128)(2,1)} %all-gather.6.cloned.1.call-done, bf16[256,1024]{1,0:T(8,128)(2,1)S(1)} %bitcast.167, bf16[256,1024]{1,0:T(8,128)(2,1)S(1)} %bitcast.166, bf16[256,1024]{1,0:T(8,128)(2,1)S(1)} %bitcast.165), kind=kOutput, calls=%fused_computation.3 | convolution fusion | flops 3226468352 | bytes 15204352 | tf_op jit(solution)/shard_map/dot_general | solution.py:91
  (94 shorter events, 52.7 us)
Async XLA Ops:
  7.2 107.2 %copy-start.13 = (bf16[256,2048]{1,0:T(8,128)(2,1)S(1)}, bf16[256,2048]{1,0:T(8,128)(2,1)}, u32[]{:S(2)}) copy-start(bf16[256,2048]{1,0:T(8,128)(2,1)} %param.11) | copy-start | bytes 3145732
  7.2 107.2 %copy-start.12 = (bf16[256,2048]{1,0:T(8,128)(2,1)S(1)}, bf16[256,2048]{1,0:T(8,128)(2,1)}, u32[]{:S(2)}) copy-start(bf16[256,2048]{1,0:T(8,128)(2,1)} %param.12) | copy-start | bytes 3145732
  7.2 107.2 %all-gather.6.cloned.1.call-start = ((), (), s32[]{:S(2)}) async-start(), calls=%async_computation | async-start | bytes 13369344 | tf_op jit(solution)/shard_map/all_gather | solution.py:50
  9.4 187.7 %all-gather.8.cloned.1.call-start = ((), (), s32[]{:S(2)}) async-start(), calls=%async_computation.1 | async-start | bytes 8912896 | tf_op jit(solution)/shard_map/all_gather | solution.py:14
  122.5 1.6 copy-start.11
  122.7 13.8 %copy-start.2 = (bf16[32,8,8,128]{3,2,1,0:T(8,128)(2,1)}, bf16[32,8,8,128]{3,2,1,0:T(8,128)(2,1)S(1)}, u32[]{:S(2)}) copy-start(bf16[32,8,8,128]{3,2,1,0:T(8,128)(2,1)S(1)} %copy.131) | copy-start | bytes 1572868
  123.9 170.7 %all-gather.10.cloned.1.call-start = ((), (), s32[]{:S(2)}) async-start(), calls=%async_computation.2 | async-start | bytes 8912896 | tf_op jit(solution)/shard_map/all_gather | solution.py:14
  128.4 0.8 copy-start.8
  131.4 5.2 %copy-start.4 = (bf16[2,128,8,128,1]{1,3,0,4,2:T(8,128)(2,1)}, bf16[2,128,8,128,1]{1,3,0,4,2:T(8,128)(2,1)S(1)}, u32[]{:S(2)}) copy-start(bf16[2,128,8,128,1]{1,3,0,4,2:T(8,128)(2,1)S(1)} %copy.101) | copy-start | bytes 1572868
  136.6 1.7 copy-start.6
  138.3 1.0 copy-start
  197.1 20.1 %copy-start.7 = (bf16[2,128,8,128]{1,3,0,2:T(8,128)(2,1)S(1)}, bf16[2,128,8,128]{1,3,0,2:T(8,128)(2,1)}, u32[]{:S(2)}) copy-start(bf16[2,128,8,128]{1,3,0,2:T(8,128)(2,1)} %copy.79) | copy-start | bytes 1572868
  225.2 8.2 %copy-start.5 = (bf16[2,128,8,128,1]{1,3,0,4,2:T(8,128)(2,1)S(1)}, bf16[2,128,8,128,1]{1,3,0,4,2:T(8,128)(2,1)}, u32[]{:S(2)}) copy-start(bf16[2,128,8,128,1]{1,3,0,4,2:T(8,128)(2,1)} %copy-done.4) | copy-start | bytes 1572868
  231.4 3.5 %copy-start.1 = (bf16[8,2,2,128,128]{3,4,1,2,0:T(8,128)(2,1)S(1)}, bf16[8,2,2,128,128]{3,4,1,2,0:T(8,128)(2,1)}, u32[]{:S(2)}) copy-start(bf16[8,2,2,128,128]{3,4,1,2,0:T(8,128)(2,1)} %copy-done) | copy-start | bytes 3145732
  294.5 20.2 %copy-start.3 = (bf16[32,8,8,128]{3,2,1,0:T(8,128)(2,1)S(1)}, bf16[32,8,8,128]{3,2,1,0:T(8,128)(2,1)}, u32[]{:S(2)}) copy-start(bf16[32,8,8,128]{3,2,1,0:T(8,128)(2,1)} %copy-done.2) | copy-start | bytes 1572868
  317.5 1.0 copy-start.9
  317.8 1.1 copy-start.10
Sparse Core Ops, SparseCore 0:
  10.9 103.4 all-gather.5
  124.0 73.0 all-gather.7
  221.4 73.1 all-gather.9
where the time goes:
time: 337 us; the launch traced here: 334 us
  waiting for transfers between devices  221 us (66%)
  other arithmetic  44.2 us (13%)
  matrix products  31.5 us (9%)
  local copies, waits for them, and re-layouts  22.9 us (7%)
  between operations  14.1 us (4%)
    all_gather x2, waiting for transfers between devices, carried_in(): everything = lax.all_gather(shard, axis)  116 us
    all_gather x1, waiting for transfers between devices, on_device(): full_weights = lax.all_gather(w_cat, 'seq', axis=0, tiled=True)  105 us
    select_n x32, other arithmetic, turn(): return jnp.where(reached, new, before)  39.4 us
    unnamed x37, local copies, waits for them, and re-layouts  9.01 us
    dot_general x1, matrix products, on_device(): lax.dot_general(d_proj, full_weights, (((1,), (1,)), ((), ())), preferred...  8.99 us
    dot_general x1, matrix products, on_device(): projected = jnp.dot(x_in, full_weights, preferred_element_type=f32)  7.98 us
  transfers between devices with their start and end apart: 3, of which 3 were waited for; matrix products, arithmetic and copies ran while one was open for 9% of the time, Pallas kernels for 0%

commit v1 on v0

--- a/solution.py
+++ b/solution.py
@@ -7,6 +7,19 @@
 DH = 128
 BLK = 128
 EPSILON = 1e-06
+
+
+def collect(array, axis, dim):
+    ways = lax.axis_size(axis)
+    up = [(d, (d + 1) % ways) for d in range(ways)]
+    down = [(d, (d - 1) % ways) for d in range(ways)]
+    earlier, later = ([array], [array])
+    for _ in range(ways // 2):
+        earlier.append(lax.ppermute(earlier[-1], axis, up))
+    for _ in range((ways - 1) // 2):
+        later.append(lax.ppermute(later[-1], axis, down))
+    line = jnp.concatenate([*earlier[::-1], *later[1:]], axis=dim)
+    return jnp.roll(line, (lax.axis_index(axis) - ways // 2) * array.shape[dim], axis=dim)
 
 
 def carried_in(shard, axis, combine, identity, reverse):
@@ -47,7 +60,7 @@
     f32 = jnp.float32
     x_in = (clean.astype(f32) + delta.astype(f32)).astype(jnp.bfloat16)
     w_cat = jnp.concatenate([w_query, w_key, w_value], axis=1)
-    full_weights = lax.all_gather(w_cat, "seq", axis=0, tiled=True)
+    full_weights = collect(w_cat, "seq", 0)
     projected = jnp.dot(x_in, full_weights, preferred_element_type=f32)
     projected = projected.astype(jnp.bfloat16)
     query = projected[:, :features].reshape(blocks_here, BLK, NH, DH)

time: 337 us -> 440 us (1.31)
  starting transfers between devices: 0.3 us -> 81.8 us
  local copies, waits for them, and re-layouts: 22.9 us -> 74.2 us
  waiting for transfers between devices: 221 us -> 188 us
  matrix products: 31.5 us -> 37 us
    all_gather x1 -> x0, waiting for transfers between devices: 105 us -> none  [on_device(): full_weights = lax.all_gather(w_cat, 'seq', axis=0, tiled=True)]
    ppermute x0 -> x15, starting transfers between devices: none -> 81.5 us  [the longest x8 75 us: collect(): earlier.append(lax.ppermute(earlier[-1], axis, up))]
    unnamed x37 -> x98, local copies, waits for them, and re-layouts: 9.01 us -> 59.9 us
    ppermute x0 -> x15, waiting for transfers between devices: none -> 50.6 us  [the longest x8 50.5 us: collect(): earlier.append(lax.ppermute(earlier[-1], axis, up))]
    all_gather x2, waiting for transfers between devices: 116 us -> 137 us  [carried_in(): everything = lax.all_gather(shard, axis)]
  transfers between devices with their start and end apart: 3 -> 17, of which waited for: 3 -> 10; matrix products, arithmetic and copies ran while one was open for 9% -> 13% of each run, Pallas kernels for 0% -> 0%
where the time goes in v1:
time: 440 us; the launch traced here: 437 us
  waiting for transfers between devices  188 us (43%)
  starting transfers between devices  81.8 us (19%)
  local copies, waits for them, and re-layouts  74.2 us (17%)
  other arithmetic  40.9 us (9%)
  matrix products  37 us (8%)
  between operations  14.5 us (3%)
    all_gather x2, waiting for transfers between devices, carried_in(): everything = lax.all_gather(shard, axis)  137 us
    ppermute x8, starting transfers between devices, collect(): earlier.append(lax.ppermute(earlier[-1], axis, up))  75 us
    unnamed x98, local copies, waits for them, and re-layouts  59.9 us
    ppermute x8, waiting for transfers between devices, collect(): earlier.append(lax.ppermute(earlier[-1], axis, up))  50.5 us
    select_n x32, other arithmetic, turn(): return jnp.where(reached, new, before)  39.3 us
    dot_general x1, matrix products, on_device(): lax.dot_general(d_proj, full_weights, (((1,), (1,)), ((), ())), preferred...  9.18 us
  transfers between devices with their start and end apart: 17, of which 10 were waited for; matrix products, arithmetic and copies ran while one was open for 13% of the time, Pallas kernels for 0%

profile of v1, /device:TPU:0, one launch (start us, length us, event | category | flops | bytes accessed | tf_op | source)
XLA Modules:
  0.0 437.0 jit_solution(2525454364516354044)
XLA Ops:
  10.7 14.7 %collective-permute-done = bf16[128,3072]{1,0:T(8,128)(2,1)S(1)} collective-permute-done((bf16[128,3072]{1,0:T(8,128)(2,1)S(1)}, bf16[128,3072]{1,0:T(8,128)(2,1)S(1)}, u32[]{:S(2)}, u32[]{:S(2)}) %collective-permute-start) | collective-permute-done | bytes 786464 | tf_op jit(solution)/shard_map/ppermute | solution.py:18
  25.3 4.4 %collective-permute-start.8 = (bf16[128,3072]{1,0:T(8,128)(2,1)S(1)}, bf16[128,3072]{1,0:T(8,128)(2,1)S(1)}, u32[]{:S(2)}, u32[]{:S(2)}) collective-permute-start(bf16[128,3072]{1,0:T(8,128)(2,1)S(1)} %constant_dynamic-update-slice_fusion), channel_id=1, source_target_pairs={{0,15},{1,0},{2,1},{3,2},{4,3},{5,4},{6,5},{7,6},{8,7},{9,8},{10,9... | collective-permute-start | bytes 2359304 | tf_op jit(solution)/shard_map/ppermute | solution.py:20
  29.8 9.8 %collective-permute-done.1 = bf16[128,3072]{1,0:T(8,128)(2,1)S(1)} collective-permute-done((bf16[128,3072]{1,0:T(8,128)(2,1)S(1)}, bf16[128,3072]{1,0:T(8,128)(2,1)S(1)}, u32[]{:S(2)}, u32[]{:S(2)}) %collective-permute-start.1) | collective-permute-done | bytes 786464 | tf_op jit(solution)/shard_map/ppermute | solution.py:18
  39.6 2.5 collective-permute-start.2
  44.0 9.8 %collective-permute-done.2 = bf16[128,3072]{1,0:T(8,128)(2,1)S(1)} collective-permute-done((bf16[128,3072]{1,0:T(8,128)(2,1)S(1)}, bf16[128,3072]{1,0:T(8,128)(2,1)S(1)}, u32[]{:S(2)}, u32[]{:S(2)}) %collective-permute-start.2) | collective-permute-done | bytes 786464 | tf_op jit(solution)/shard_map/ppermute | solution.py:18
  53.8 7.4 %collective-permute-start.3 = (bf16[128,3072]{1,0:T(8,128)(2,1)S(1)}, bf16[128,3072]{1,0:T(8,128)(2,1)S(1)}, u32[]{:S(2)}, u32[]{:S(2)}) collective-permute-start(bf16[128,3072]{1,0:T(8,128)(2,1)S(1)} %collective-permute-done.2), channel_id=1, source_target_pairs={{0,1},{1,2},{2,3},{3,4},{4,5},{5,6},{6,7},{7,8},{8,9},{9,10},{10,1... | collective-permute-start | bytes 2359304 | tf_op jit(solution)/shard_map/ppermute | solution.py:18
  61.2 6.8 %collective-permute-done.3 = bf16[128,3072]{1,0:T(8,128)(2,1)S(1)} collective-permute-done((bf16[128,3072]{1,0:T(8,128)(2,1)S(1)}, bf16[128,3072]{1,0:T(8,128)(2,1)S(1)}, u32[]{:S(2)}, u32[]{:S(2)}) %collective-permute-start.3) | collective-permute-done | bytes 786464 | tf_op jit(solution)/shard_map/ppermute | solution.py:18
  68.0 13.0 %collective-permute-start.4 = (bf16[128,3072]{1,0:T(8,128)(2,1)S(1)}, bf16[128,3072]{1,0:T(8,128)(2,1)S(1)}, u32[]{:S(2)}, u32[]{:S(2)}) collective-permute-start(bf16[128,3072]{1,0:T(8,128)(2,1)S(1)} %collective-permute-done.3), channel_id=1, source_target_pairs={{0,1},{1,2},{2,3},{3,4},{4,5},{5,6},{6,7},{7,8},{8,9},{9,10},{10,1... | collective-permute-start | bytes 2359304 | tf_op jit(solution)/shard_map/ppermute | solution.py:18
  83.3 17.6 %collective-permute-start.5 = (bf16[128,3072]{1,0:T(8,128)(2,1)S(1)}, bf16[128,3072]{1,0:T(8,128)(2,1)S(1)}, u32[]{:S(2)}, u32[]{:S(2)}) collective-permute-start(bf16[128,3072]{1,0:T(8,128)(2,1)S(1)} %collective-permute-done.4), channel_id=1, source_target_pairs={{0,1},{1,2},{2,3},{3,4},{4,5},{5,6},{6,7},{7,8},{8,9},{9,10},{10,1... | collective-permute-start | bytes 2359304 | tf_op jit(solution)/shard_map/ppermute | solution.py:18
  103.2 17.5 %collective-permute-start.6 = (bf16[128,3072]{1,0:T(8,128)(2,1)S(1)}, bf16[128,3072]{1,0:T(8,128)(2,1)}, u32[]{:S(2)}, u32[]{:S(2)}) collective-permute-start(bf16[128,3072]{1,0:T(8,128)(2,1)S(1)} %collective-permute-done.5), channel_id=1, source_target_pairs={{0,1},{1,2},{2,3},{3,4},{4,5},{5,6},{6,7},{7,8},{8,9},{9,10},{10,1... | collective-permute-start | bytes 2359304 | tf_op jit(solution)/shard_map/ppermute | solution.py:18
  120.7 3.3 collective-permute-done.6
  124.0 16.6 %collective-permute-start.7 = (bf16[128,3072]{1,0:T(8,128)(2,1)}, bf16[128,3072]{1,0:T(8,128)(2,1)}, u32[]{:S(2)}, u32[]{:S(2)}) collective-permute-start(bf16[128,3072]{1,0:T(8,128)(2,1)} %collective-permute-done.6), channel_id=1, source_target_pairs={{0,1},{1,2},{2,3},{3,4},{4,5},{5,6},{6,7},{7,8},{8,9},{9,10},{10,1... | collective-permute-start | bytes 2359304 | tf_op jit(solution)/shard_map/ppermute | solution.py:18
  140.7 3.4 collective-permute-done.7
  167.6 2.1 constant_dynamic-update-slice_fusion.22
  195.9 8.1 %fusion.4 = bf16[256,3072]{1,0:T(8,128)(2,1)S(1)} fusion(bf16[4096,3072]{1,0:T(8,128)(2,1)} %constant_dynamic-update-slice_fusion.3, s32[]{:T(128)S(6)} %select_n.65, bf16[256,2048]{1,0:T(8,128)(2,1)S(1)} %copy-done.24, bf16[256,2048]{1,0:T(8,128)(2,1)S(1)} %copy-done.25), kind=kOutput, calls=%fused_computation.6 | convolution fusion | flops 3224109056 | bytes 16252932 | tf_op jit(solution)/shard_map/dot_general | solution.py:64
  213.0 2.1 copy.96
  215.1 2.1 copy.79
  220.3 77.7 %all-gather.5.cloned.1.call-done = f32[128,128,128]{2,1,0:T(8,128)} async-done(((f32[8,128,128]{2,1,0:T(8,128)}), f32[128,128,128]{2,1,0:T(8,128)}) %all-gather.5.cloned.1.call-update) | async-done | bytes 8388624 | tf_op jit(solution)/shard_map/all_gather | solution.py:27
  298.0 20.0 %while.30 = (s32[]{:T(128)}, f32[8,128,128]{2,1,0:T(8,128)S(1)}, s32[]{:T(128)}, f32[16,8,128,128]{3,2,1,0:T(8,128)}, s32[]{:T(128)}, /*index=5*/s32[]{:T(128)}) while((s32[]{:T(128)}, f32[8,128,128]{2,1,0:T(8,128)S(1)}, s32[]{:T(128)}, f32[16,8,128,128]{3,2,1,0:T(8,128)}, s32[]{:T(128)}, /*index=5*/s32[]{:T(128)}) %tuple.87), condition=%wide.region_1.2_spmd.clone, body=%wide.region_0.1_spmd.clone.sunk | while | flops 393220 | bytes 1572957 | solution.py:36
  321.2 2.2 convolution_bitcast_fusion.4
  332.9 2.9 convolution_bitcast_fusion.2
  337.2 59.6 %all-gather.7.cloned.1.call-done = f32[128,128,128]{2,1,0:T(8,128)} async-done(((f32[8,128,128]{2,1,0:T(8,128)}), f32[128,128,128]{2,1,0:T(8,128)}) %all-gather.7.cloned.1.call-update) | async-done | bytes 8388624 | tf_op jit(solution)/shard_map/all_gather | solution.py:27
  396.7 20.1 %while.31 = (s32[]{:T(128)}, f32[8,128,128]{2,1,0:T(8,128)S(1)}, s32[]{:T(128)}, f32[16,8,128,128]{3,2,1,0:T(8,128)}, s32[]{:T(128)}, /*index=5*/s32[]{:T(128)}, s32[]{:T(128)}, s32[]{:T(128)}) while((s32[]{:T(128)}, f32[8,128,128]{2,1,0:T(8,128)S(1)}, s32[]{:T(128)}, f32[16,8,128,128]{3,2,1,0:T(8,128)}, s32[]{:T(128)}, ...), condition=%wide.region_5.6_spmd.clone, body=%wide.region_4.5_spmd.clone.sunk | while | flops 393224 | bytes 1573019 | solution.py:36
  420.9 9.2 %fusion.7 = bf16[256,2048]{1,0:T(8,128)(2,1)} fusion(bf16[4096,3072]{1,0:T(8,128)(2,1)} %constant_dynamic-update-slice_fusion.3, s32[]{:T(128)S(6)} %select_n.65, bf16[256,1024]{1,0:T(8,128)(2,1)S(1)} %bitcast.165, bf16[256,1024]{1,0:T(8,128)(2,1)S(1)} %bitcast.164, bf16[256,1024]{1,0:T(8,128)(2,1)} %bitcast.163), kind=kOutput, calls=%fused_computation.7 | convolution fusion | flops 3226468352 | bytes 15204356 | tf_op jit(solution)/shard_map/dot_general | solution.py:104
  (183 shorter events, 129.0 us)
Async XLA Ops:
  7.2 177.6 %copy-start.19 = (bf16[128,1024]{1,0:T(8,128)(2,1)S(1)}, bf16[128,1024]{1,0:T(8,128)(2,1)}, u32[]{:S(2)}) copy-start(bf16[128,1024]{1,0:T(8,128)(2,1)} %param.14) | copy-start | bytes 786436
  7.2 290.8 %all-gather.5.cloned.1.call-start = ((), (), s32[]{:S(2)}) async-start(), calls=%async_computation | async-start | bytes 8912896 | tf_op jit(solution)/shard_map/all_gather | solution.py:27
  10.2 15.2 %collective-permute-start = (bf16[128,3072]{1,0:T(8,128)(2,1)S(1)}, bf16[128,3072]{1,0:T(8,128)(2,1)S(1)}, u32[]{:S(2)}, u32[]{:S(2)}) collective-permute-start(bf16[128,3072]{1,0:T(8,128)(2,1)S(1)} %constant_dynamic-update-slice_fusion), channel_id=1, source_target_pairs={{0,1},{1,2},{2,3},{3,4},{4,5},{5,6},{6,7},{7,8},{8,9},{9,10},{10,1... | collective-permute-start | bytes 2359304 | tf_op jit(solution)/shard_map/ppermute | solution.py:18
  25.3 14.2 %collective-permute-start.1 = (bf16[128,3072]{1,0:T(8,128)(2,1)S(1)}, bf16[128,3072]{1,0:T(8,128)(2,1)S(1)}, u32[]{:S(2)}, u32[]{:S(2)}) collective-permute-start(bf16[128,3072]{1,0:T(8,128)(2,1)S(1)} %collective-permute-done), channel_id=1, source_target_pairs={{0,1},{1,2},{2,3},{3,4},{4,5},{5,6},{6,7},{7,8},{8,9},{9,10},{10,1... | collective-permute-start | bytes 2359304 | tf_op jit(solution)/shard_map/ppermute | solution.py:18
  25.3 16.7 %collective-permute-start.8 = (bf16[128,3072]{1,0:T(8,128)(2,1)S(1)}, bf16[128,3072]{1,0:T(8,128)(2,1)S(1)}, u32[]{:S(2)}, u32[]{:S(2)}) collective-permute-start(bf16[128,3072]{1,0:T(8,128)(2,1)S(1)} %constant_dynamic-update-slice_fusion), channel_id=1, source_target_pairs={{0,15},{1,0},{2,1},{3,2},{4,3},{5,4},{6,5},{7,6},{8,7},{9,8},{10,9... | collective-permute-start | bytes 2359304 | tf_op jit(solution)/shard_map/ppermute | solution.py:20
  39.6 14.2 %collective-permute-start.2 = (bf16[128,3072]{1,0:T(8,128)(2,1)S(1)}, bf16[128,3072]{1,0:T(8,128)(2,1)S(1)}, u32[]{:S(2)}, u32[]{:S(2)}) collective-permute-start(bf16[128,3072]{1,0:T(8,128)(2,1)S(1)} %collective-permute-done.1), channel_id=1, source_target_pairs={{0,1},{1,2},{2,3},{3,4},{4,5},{5,6},{6,7},{7,8},{8,9},{9,10},{10,1... | collective-permute-start | bytes 2359304 | tf_op jit(solution)/shard_map/ppermute | solution.py:18
  42.1 19.1 %collective-permute-start.9 = (bf16[128,3072]{1,0:T(8,128)(2,1)S(1)}, bf16[128,3072]{1,0:T(8,128)(2,1)S(1)}, u32[]{:S(2)}, u32[]{:S(2)}) collective-permute-start(bf16[128,3072]{1,0:T(8,128)(2,1)S(1)} %collective-permute-done.8), channel_id=1, source_target_pairs={{0,15},{1,0},{2,1},{3,2},{4,3},{5,4},{6,5},{7,6},{8,7},{9,8},{10,9... | collective-permute-start | bytes 2359304 | tf_op jit(solution)/shard_map/ppermute | solution.py:20
  53.8 14.2 %collective-permute-start.3 = (bf16[128,3072]{1,0:T(8,128)(2,1)S(1)}, bf16[128,3072]{1,0:T(8,128)(2,1)S(1)}, u32[]{:S(2)}, u32[]{:S(2)}) collective-permute-start(bf16[128,3072]{1,0:T(8,128)(2,1)S(1)} %collective-permute-done.2), channel_id=1, source_target_pairs={{0,1},{1,2},{2,3},{3,4},{4,5},{5,6},{6,7},{7,8},{8,9},{9,10},{10,1... | collective-permute-start | bytes 2359304 | tf_op jit(solution)/shard_map/ppermute | solution.py:18
  61.2 19.8 %collective-permute-start.10 = (bf16[128,3072]{1,0:T(8,128)(2,1)S(1)}, bf16[128,3072]{1,0:T(8,128)(2,1)S(1)}, u32[]{:S(2)}, u32[]{:S(2)}) collective-permute-start(bf16[128,3072]{1,0:T(8,128)(2,1)S(1)} %collective-permute-done.9), channel_id=1, source_target_pairs={{0,15},{1,0},{2,1},{3,2},{4,3},{5,4},{6,5},{7,6},{8,7},{9,8},{10,9... | collective-permute-start | bytes 2359304 | tf_op jit(solution)/shard_map/ppermute | solution.py:20
  68.0 52.7 %copy-start.13 = (bf16[128,3072]{1,0:T(8,128)(2,1)}, bf16[128,3072]{1,0:T(8,128)(2,1)S(1)}, u32[]{:S(2)}) copy-start(bf16[128,3072]{1,0:T(8,128)(2,1)S(1)} %collective-permute-done.3) | copy-start | bytes 2359300
  68.0 15.3 %collective-permute-start.4 = (bf16[128,3072]{1,0:T(8,128)(2,1)S(1)}, bf16[128,3072]{1,0:T(8,128)(2,1)S(1)}, u32[]{:S(2)}, u32[]{:S(2)}) collective-permute-start(bf16[128,3072]{1,0:T(8,128)(2,1)S(1)} %collective-permute-done.3), channel_id=1, source_target_pairs={{0,1},{1,2},{2,3},{3,4},{4,5},{5,6},{6,7},{7,8},{8,9},{9,10},{10,1... | collective-permute-start | bytes 2359304 | tf_op jit(solution)/shard_map/ppermute | solution.py:18
  81.0 19.8 %collective-permute-start.11 = (bf16[128,3072]{1,0:T(8,128)(2,1)S(1)}, bf16[128,3072]{1,0:T(8,128)(2,1)S(1)}, u32[]{:S(2)}, u32[]{:S(2)}) collective-permute-start(bf16[128,3072]{1,0:T(8,128)(2,1)S(1)} %collective-permute-done.10), channel_id=1, source_target_pairs={{0,15},{1,0},{2,1},{3,2},{4,3},{5,4},{6,5},{7,6},{8,7},{9,8},{10,9... | collective-permute-start | bytes 2359304 | tf_op jit(solution)/shard_map/ppermute | solution.py:20
  83.3 19.9 %collective-permute-start.5 = (bf16[128,3072]{1,0:T(8,128)(2,1)S(1)}, bf16[128,3072]{1,0:T(8,128)(2,1)S(1)}, u32[]{:S(2)}, u32[]{:S(2)}) collective-permute-start(bf16[128,3072]{1,0:T(8,128)(2,1)S(1)} %collective-permute-done.4), channel_id=1, source_target_pairs={{0,1},{1,2},{2,3},{3,4},{4,5},{5,6},{6,7},{7,8},{8,9},{9,10},{10,1... | collective-permute-start | bytes 2359304 | tf_op jit(solution)/shard_map/ppermute | solution.py:18
  101.7 19.0 %collective-permute-start.12 = (bf16[128,3072]{1,0:T(8,128)(2,1)S(1)}, bf16[128,3072]{1,0:T(8,128)(2,1)}, u32[]{:S(2)}, u32[]{:S(2)}) collective-permute-start(bf16[128,3072]{1,0:T(8,128)(2,1)S(1)} %collective-permute-done.11), channel_id=1, source_target_pairs={{0,15},{1,0},{2,1},{3,2},{4,3},{5,4},{6,5},{7,6},{8,7},{9,8},{10,9... | collective-permute-start | bytes 2359304 | tf_op jit(solution)/shard_map/ppermute | solution.py:20
  103.2 20.8 %collective-permute-start.6 = (bf16[128,3072]{1,0:T(8,128)(2,1)S(1)}, bf16[128,3072]{1,0:T(8,128)(2,1)}, u32[]{:S(2)}, u32[]{:S(2)}) collective-permute-start(bf16[128,3072]{1,0:T(8,128)(2,1)S(1)} %collective-permute-done.5), channel_id=1, source_target_pairs={{0,1},{1,2},{2,3},{3,4},{4,5},{5,6},{6,7},{7,8},{8,9},{9,10},{10,1... | collective-permute-start | bytes 2359304 | tf_op jit(solution)/shard_map/ppermute | solution.py:18
  120.7 19.9 %collective-permute-start.13 = (bf16[128,3072]{1,0:T(8,128)(2,1)}, bf16[128,3072]{1,0:T(8,128)(2,1)}, u32[]{:S(2)}, u32[]{:S(2)}) collective-permute-start(bf16[128,3072]{1,0:T(8,128)(2,1)} %collective-permute-done.12), channel_id=1, source_target_pairs={{0,15},{1,0},{2,1},{3,2},{4,3},{5,4},{6,5},{7,6},{8,7},{9,8},{10,9... | collective-permute-start | bytes 2359304 | tf_op jit(solution)/shard_map/ppermute | solution.py:20
  124.0 20.1 %collective-permute-start.7 = (bf16[128,3072]{1,0:T(8,128)(2,1)}, bf16[128,3072]{1,0:T(8,128)(2,1)}, u32[]{:S(2)}, u32[]{:S(2)}) collective-permute-start(bf16[128,3072]{1,0:T(8,128)(2,1)} %collective-permute-done.6), channel_id=1, source_target_pairs={{0,1},{1,2},{2,3},{3,4},{4,5},{5,6},{6,7},{7,8},{8,9},{9,10},{10,1... | collective-permute-start | bytes 2359304 | tf_op jit(solution)/shard_map/ppermute | solution.py:18
  140.6 49.2 %copy-start.12 = (bf16[128,3072]{1,0:T(8,128)(2,1)S(1)}, bf16[128,3072]{1,0:T(8,128)(2,1)}, u32[]{:S(2)}) copy-start(bf16[128,3072]{1,0:T(8,128)(2,1)} %copy-done.11) | copy-start | bytes 2359300
  140.6 55.3 %copy-start.24 = (bf16[256,2048]{1,0:T(8,128)(2,1)S(1)}, bf16[256,2048]{1,0:T(8,128)(2,1)}, u32[]{:S(2)}) copy-start(bf16[256,2048]{1,0:T(8,128)(2,1)} %param.12) | copy-start | bytes 3145732
  140.6 55.3 %copy-start.25 = (bf16[256,2048]{1,0:T(8,128)(2,1)S(1)}, bf16[256,2048]{1,0:T(8,128)(2,1)}, u32[]{:S(2)}) copy-start(bf16[256,2048]{1,0:T(8,128)(2,1)} %param.11) | copy-start | bytes 3145732
  140.6 33.3 %collective-permute-start.14 = (bf16[128,3072]{1,0:T(8,128)(2,1)}, bf16[128,3072]{1,0:T(8,128)(2,1)S(1)}, u32[]{:S(2)}, u32[]{:S(2)}) collective-permute-start(bf16[128,3072]{1,0:T(8,128)(2,1)} %collective-permute-done.13), channel_id=1, source_target_pairs={{0,15},{1,0},{2,1},{3,2},{4,3},{5,4},{6,5},{7,6},{8,7},{9,8},{10,9... | collective-permute-start | bytes 2359304 | tf_op jit(solution)/shard_map/ppermute | solution.py:20
  205.6 191.1 %all-gather.7.cloned.1.call-start = ((), (), s32[]{:S(2)}) async-start(), calls=%async_computation.1 | async-start | bytes 8912896 | tf_op jit(solution)/shard_map/all_gather | solution.py:27
  212.1 108.0 %copy-start.4 = (bf16[2,128,8,128,1]{1,3,0,4,2:T(8,128)(2,1)}, bf16[2,128,8,128,1]{1,3,0,4,2:T(8,128)(2,1)S(1)}, u32[]{:S(2)}) copy-start(bf16[2,128,8,128,1]{1,3,0,4,2:T(8,128)(2,1)S(1)} %copy.101) | copy-start | bytes 1572868
  321.2 95.6 %copy-start.3 = (bf16[32,8,8,128]{3,2,1,0:T(8,128)(2,1)S(1)}, bf16[32,8,8,128]{3,2,1,0:T(8,128)(2,1)}, u32[]{:S(2)}) copy-start(bf16[32,8,8,128]{3,2,1,0:T(8,128)(2,1)} %copy-done.2) | copy-start | bytes 1572868
  (19 other events, 434.8 us)
Sparse Core Ops, SparseCore 0:
  205.7 92.2 all-gather.4
  323.5 73.1 all-gather.6
